TPU v7x, 512 devices: a whole 4x8x8 slice. The times are simulated.
512 devices in a mesh: chan: 16 (over y, core), tm: 32 (over z, x).
Axes of the slice: x: 4, y: 8, z: 8, core: 2. Of those that a mesh axis runs over, the one named last changes fastest.
Arguments:
- spike_sample: int32 [16, 131072], P('chan', 'tm'), may hold values from 0 to 245759, as said below
- spike_unit: int32 [16, 131072], P('chan', 'tm'), may hold values from 0 to 6143, as said below
- spike_amp: bfloat16 [16, 131072], P('chan', 'tm'), may hold values from 0.2 to 12, as said below
- pair_units: int32 [2, 16384], P(None, 'chan'), may hold values from 0 to 6143, as said below
Outputs:
- corr: float32 [101, 16384], P(None, ('chan', 'tm'))
Inputs may be any that keep to these rules, and one draw needn't show every extreme that they name: `spike_sample`: the spike in column c of a row lies in time shard s = c // 4096: its sample index is at least s * 256 * 30 and below (s + 1) * 256 * 30. `spike_unit`: row g holds only spikes of units g * 384 to (g + 1) * 384 - 1. `spike_amp`: amplitudes are positive. `pair_units`: column c belongs to group g = c // 1024: its first unit is a unit of group g; its second is a unit of group g or, unless g is the last group, one of the first 64 units of group g + 1.
All inputs are finite; a program needn't handle non-finite values.
Results may differ from a plain program's by a relative error of at most 0.0031.
Values may be sent and summed in bfloat16 or wider, within the bound.
No kernel may reach another device: no remote copies, remote signals or barrier semaphores. Data moves between devices by JAX's collectives and lax.ppermute only.
A program may use at most 64 MiB of HBM per device.

v0:
```python
import math
import jax
import jax.numpy as jnp
from jax import lax
from jax.sharding import PartitionSpec as P

U_GRP = 384
BORDER = 64
BINS_DEV = 256
MAXLAG = 50
SPB = 30


def passed_along(array, axis, by):
    peers = lax.axis_size(axis)
    pairs = [(i, i + by) for i in range(peers) if 0 <= i + by < peers]
    return lax.ppermute(array, axis, pairs)


def extended_2(cells, sides, width):
    for axis, dim in sides:
        count = lax.axis_size(axis)
        ends = count - 1
        head = lax.slice_in_dim(cells, 0, width, axis=dim)
        tail = lax.slice_in_dim(cells, cells.shape[dim] - width, cells.shape[dim], axis=dim)
        cells = jnp.concatenate(
            [
                lax.ppermute(tail, axis, [(i, (i + 1) % count) for i in range(ends)]),
                cells,
                lax.ppermute(head, axis, [((i + 1) % count, i) for i in range(ends)]),
            ],
            axis=dim,
        )
    return cells


def lag_window(left_rows, right_rows):
    width = left_rows.shape[1]
    windows = jnp.stack([right_rows[:, k : k + width] for k in range(2 * MAXLAG + 1)], axis=1)
    return jnp.einsum("nt,nlt->nl", left_rows, windows, preferred_element_type=jnp.float32)


def pair_terms(centred, padded, first_units, second_units):
    total_pairs = first_units.shape[0]
    block_rows = math.gcd(total_pairs, 256)

    def one_block(indices):
        return lag_window(
            jnp.take(centred, indices[0], axis=0), jnp.take(padded, indices[1], axis=0)
        )

    results = lax.map(
        one_block, (first_units.reshape(-1, block_rows), second_units.reshape(-1, block_rows))
    )
    return results.reshape(total_pairs, -1).T


def shard_prelude(spike_sample, spike_unit, spike_amp, group_index, shard_index, shard_count):
    bin_index = spike_sample[0] // SPB - shard_index * BINS_DEV
    within = spike_unit[0] - group_index * U_GRP
    unit_onehot = (within[None, :] == jnp.arange(U_GRP, dtype=jnp.int32)[:, None]).astype(
        jnp.bfloat16
    )
    weighted = jnp.where(
        bin_index[:, None] == jnp.arange(BINS_DEV, dtype=jnp.int32)[None, :],
        spike_amp[0][:, None],
        jnp.zeros((), jnp.bfloat16),
    )
    trains = jnp.dot(unit_onehot, weighted, preferred_element_type=jnp.float32)
    totals = lax.psum(jnp.sum(trains, axis=1), "tm")
    means = totals / float(BINS_DEV * shard_count)
    centred = (trains - means[:, None]).astype(jnp.bfloat16)
    border_rows = passed_along(centred[:BORDER], "chan", -1)
    extended = jnp.concatenate([centred, border_rows], axis=0)
    padded = extended_2(extended, (("tm", 1),), MAXLAG)
    return (centred, padded)


def local(spike_sample, spike_unit, spike_amp, pair_units):
    group_index = lax.axis_index("chan")
    shard_index = lax.axis_index("tm")
    shard_count = lax.axis_size("tm")
    first_units = pair_units[0] - group_index * U_GRP
    second_units = pair_units[1] - group_index * U_GRP
    per_shard = first_units.shape[0] // shard_count
    centred, padded = shard_prelude(
        spike_sample, spike_unit, spike_amp, group_index, shard_index, shard_count
    )
    summed = lax.psum(pair_terms(centred, padded, first_units, second_units), "tm")
    return lax.dynamic_slice_in_dim(summed, shard_index * per_shard, per_shard, 1)


def solution(mesh):
    in_specs = (P("chan", "tm"), P("chan", "tm"), P("chan", "tm"), P(None, "chan"))
    out_specs = P(None, ("chan", "tm"))
    return jax.shard_map(local, mesh=mesh, in_specs=in_specs, out_specs=out_specs, check_vma=False)
```

profile of v0, /device:TPU:8, one launch (start us, length us, event | category | flops | bytes accessed | tf_op | source)
XLA Modules:
  0.0 395.8 jit_solution(884954820506347946)
XLA Ops:
  6.5 0.8 broadcast_divide_fusion
  7.3 0.8 and_reduce_fusion
  8.1 0.7 broadcast_subtract_fusion
  8.9 0.8 reduce.2
  9.7 1.7 fusion.13
  11.3 80.8 %psum.14 = f32[384]{0:T(512)S(1)} all-reduce(f32[384]{0:T(512)S(1)} %get-tuple-element.60), channel_id=1, replica_groups=mesh['chan'=16,'tm'=32] {'tm'}, use_global_device_ids=true, to_apply=%region_1.2 | all-reduce | flops 384 | bytes 3072 | tf_op jit(solution)/shard_map/psum | solution.py:70
  92.2 0.1 subtract_convert_fusion
  92.3 1.9 collective-permute-start
  94.3 1.6 collective-permute-done
  95.9 1.3 collective-permute-start.1
  97.2 1.3 collective-permute-start.2
  98.5 0.8 subtract_reduce_fusion
  99.4 0.4 collective-permute-done.1
  99.8 4.7 %collective-permute-done.2 = bf16[448,50]{1,0:T(8,128)(2,1)S(1)} collective-permute-done((bf16[448,50]{1,0:T(8,128)(2,1)S(1)}, bf16[448,50]{1,0:T(8,128)(2,1)S(1)}, u32[]{:S(2)}, u32[]{:S(2)}) %collective-permute-start.2) | collective-permute-done | bytes 44832 | tf_op jit(solution)/shard_map/ppermute | solution.py:30
  104.5 0.2 pad_maximum_fusion
  104.7 124.1 %while.10 = (s32[]{:T(128)}, f32[4,256,101]{2,1,0:T(8,128)}, s32[4,256]{1,0:T(4,128)S(1)}, bf16[384,256]{1,0:T(8,128)(2,1)S(1)}, s32[4,256]{1,0:T(4,128)S(1)}, /*index=5*/bf16[448,356]{1,0:T(8,128)(2,1)S(1)}, s32[]{:T(128)}) while((s32[]{:T(128)}, f32[4,256,101]{2,1,0:T(8,128)}, s32[4,256]{1,0:T(4,128)S(1)}, bf16[384,256]{1,0:T(8,128)(2,1)S(1)}, ...), condition=%wide.region_3.4_spmd, body=%wide.region_2.3_spmd.sunk | while | flops 13401602 | bytes 94412400 | solution.py:52
  104.9 1.2 gather_fusion
  106.1 0.1 broadcast_select_fusion.2
  106.9 0.1 constant_dynamic-update-slice_fusion.209
  107.0 0.1 constant_dynamic-update-slice_fusion.210
  107.1 0.1 constant_dynamic-update-slice_fusion.211
  107.2 0.1 constant_dynamic-update-slice_fusion.212
  107.3 0.1 constant_dynamic-update-slice_fusion.213
  107.5 0.1 constant_dynamic-update-slice_fusion.214
  117.4 4.7 %copy-done = bf16[256,101,256]{2,0,1:T(8,128)(2,1)} copy-done((bf16[256,101,256]{2,0,1:T(8,128)(2,1)}, bf16[256,101,256]{2,0,1:T(8,128)(2,1)S(1)}, u32[]{:S(2)}) %copy-start) | copy-done | bytes 13238296 | tf_op jit(solution)/shard_map/while
  122.1 1.1 gather_fusion.1
  123.4 11.8 %fusion.19 = f32[256,1,101]{2,1,0:T(1,128)S(1)} fusion(bf16[256,101,256]{2,0,1:T(8,128)(2,1)} %copy-done, bf16[256,256,1]{1,0,2:T(8,128)(2,1)S(1)} %select_bitcast_fusion.2), kind=kOutput, calls=%fused_computation.2.clone.1 | convolution fusion | flops 13238272 | bytes 13472768 | tf_op jit(solution)/shard_map/while/body/eval_jaxpr/nt,nlt->nl/dot_general | solution.py:40
  135.2 0.7 bitcast_dynamic-update-slice_fusion.2
  135.9 1.2 gather_fusion
  137.1 0.1 broadcast_select_fusion.2
  148.4 4.7 %copy-done = bf16[256,101,256]{2,0,1:T(8,128)(2,1)} copy-done((bf16[256,101,256]{2,0,1:T(8,128)(2,1)}, bf16[256,101,256]{2,0,1:T(8,128)(2,1)S(1)}, u32[]{:S(2)}) %copy-start) | copy-done | bytes 13238296 | tf_op jit(solution)/shard_map/while
  153.1 1.1 gather_fusion.1
  154.3 11.8 %fusion.19 = f32[256,1,101]{2,1,0:T(1,128)S(1)} fusion(bf16[256,101,256]{2,0,1:T(8,128)(2,1)} %copy-done, bf16[256,256,1]{1,0,2:T(8,128)(2,1)S(1)} %select_bitcast_fusion.2), kind=kOutput, calls=%fused_computation.2.clone.1 | convolution fusion | flops 13238272 | bytes 13472768 | tf_op jit(solution)/shard_map/while/body/eval_jaxpr/nt,nlt->nl/dot_general | solution.py:40
  166.2 0.7 bitcast_dynamic-update-slice_fusion.2
  166.9 1.2 gather_fusion
  168.1 0.1 broadcast_select_fusion.2
  179.4 4.7 %copy-done = bf16[256,101,256]{2,0,1:T(8,128)(2,1)} copy-done((bf16[256,101,256]{2,0,1:T(8,128)(2,1)}, bf16[256,101,256]{2,0,1:T(8,128)(2,1)S(1)}, u32[]{:S(2)}) %copy-start) | copy-done | bytes 13238296 | tf_op jit(solution)/shard_map/while
  184.0 1.1 gather_fusion.1
  185.3 11.8 %fusion.19 = f32[256,1,101]{2,1,0:T(1,128)S(1)} fusion(bf16[256,101,256]{2,0,1:T(8,128)(2,1)} %copy-done, bf16[256,256,1]{1,0,2:T(8,128)(2,1)S(1)} %select_bitcast_fusion.2), kind=kOutput, calls=%fused_computation.2.clone.1 | convolution fusion | flops 13238272 | bytes 13472768 | tf_op jit(solution)/shard_map/while/body/eval_jaxpr/nt,nlt->nl/dot_general | solution.py:40
  197.2 0.7 bitcast_dynamic-update-slice_fusion.2
  197.9 1.2 gather_fusion
  199.0 0.1 broadcast_select_fusion.2
  210.3 4.7 %copy-done = bf16[256,101,256]{2,0,1:T(8,128)(2,1)} copy-done((bf16[256,101,256]{2,0,1:T(8,128)(2,1)}, bf16[256,101,256]{2,0,1:T(8,128)(2,1)S(1)}, u32[]{:S(2)}) %copy-start) | copy-done | bytes 13238296 | tf_op jit(solution)/shard_map/while
  215.0 1.1 gather_fusion.1
  216.3 11.8 %fusion.19 = f32[256,1,101]{2,1,0:T(1,128)S(1)} fusion(bf16[256,101,256]{2,0,1:T(8,128)(2,1)} %copy-done, bf16[256,256,1]{1,0,2:T(8,128)(2,1)S(1)} %select_bitcast_fusion.2), kind=kOutput, calls=%fused_computation.2.clone.1 | convolution fusion | flops 13238272 | bytes 13472768 | tf_op jit(solution)/shard_map/while/body/eval_jaxpr/nt,nlt->nl/dot_general | solution.py:40
  228.2 0.7 bitcast_dynamic-update-slice_fusion.2
  228.8 158.8 %all-reduce.2.cloned.1.call-done = f32[101,1024]{0,1:T(8,128)} async-done(((f32[101,1024]{0,1:T(8,128)}), f32[101,1024]{0,1:T(8,128)}) %all-reduce.2.cloned.1.call-update) | async-done | bytes 413712 | tf_op jit(solution)/shard_map/psum | solution.py:89
  387.6 1.3 constant_dynamic-slice_fusion.2
  (435 shorter events, 41.8 us)
Async XLA Ops:
  6.5 381.1 %all-reduce.2.cloned.1.call-start = ((), (), s32[]{:S(2)}) async-start(), calls=%async_computation | async-start | bytes 1048576 | tf_op jit(solution)/shard_map/psum | solution.py:89
  92.3 3.5 collective-permute-start
  95.9 3.8 collective-permute-start.1
  97.2 7.2 %collective-permute-start.2 = (bf16[448,50]{1,0:T(8,128)(2,1)S(1)}, bf16[448,50]{1,0:T(8,128)(2,1)S(1)}, u32[]{:S(2)}, u32[]{:S(2)}) collective-permute-start(bf16[448,50]{1,0:T(8,128)(2,1)S(1)} %get-tuple-element.59), channel_id=1, source_target_pairs={{1,0},{2,1},{3,2},{4,3},{5,4},{6,5},{7,6},{8,7},{9,8},{10,9},{11,1... | collective-permute-start | bytes 134408 | tf_op jit(solution)/shard_map/ppermute | solution.py:30
  117.4 4.7 %copy-start = (bf16[256,101,256]{2,0,1:T(8,128)(2,1)}, bf16[256,101,256]{2,0,1:T(8,128)(2,1)S(1)}, u32[]{:S(2)}) copy-start(bf16[256,101,256]{2,0,1:T(8,128)(2,1)S(1)} %constant_dynamic-update-slice_fusion.302) | copy-start | bytes 39714820 | tf_op jit(solution)/shard_map/while
  148.4 4.7 %copy-start = (bf16[256,101,256]{2,0,1:T(8,128)(2,1)}, bf16[256,101,256]{2,0,1:T(8,128)(2,1)S(1)}, u32[]{:S(2)}) copy-start(bf16[256,101,256]{2,0,1:T(8,128)(2,1)S(1)} %constant_dynamic-update-slice_fusion.302) | copy-start | bytes 39714820 | tf_op jit(solution)/shard_map/while
  179.3 4.7 %copy-start = (bf16[256,101,256]{2,0,1:T(8,128)(2,1)}, bf16[256,101,256]{2,0,1:T(8,128)(2,1)S(1)}, u32[]{:S(2)}) copy-start(bf16[256,101,256]{2,0,1:T(8,128)(2,1)S(1)} %constant_dynamic-update-slice_fusion.302) | copy-start | bytes 39714820 | tf_op jit(solution)/shard_map/while
  210.3 4.7 %copy-start = (bf16[256,101,256]{2,0,1:T(8,128)(2,1)}, bf16[256,101,256]{2,0,1:T(8,128)(2,1)S(1)}, u32[]{:S(2)}) copy-start(bf16[256,101,256]{2,0,1:T(8,128)(2,1)S(1)} %constant_dynamic-update-slice_fusion.302) | copy-start | bytes 39714820 | tf_op jit(solution)/shard_map/while
Sparse Core Ops, SparseCore 0:
  229.0 158.6 all-reduce.1
where the time goes:
time: 397 us; the launch traced here: 396 us
  waiting for transfers between devices  165 us (42%)
  blocking collectives  80.8 us (20%)
  local copies, waits for them, and re-layouts  73.7 us (19%)
  matrix products  49.1 us (12%)
  between operations  13.5 us (3%)
  other arithmetic  5.34 us (1%)
  starting transfers between devices  4.51 us (1%)
    psum x1, waiting for transfers between devices, local(): lax.psum(pair_terms(centred, padded, first_units, second_units), 'tm')  159 us
    psum x1, blocking collectives, shard_prelude(): totals = lax.psum(jnp.sum(trains, axis=1), 'tm')  80.8 us
    while x408, local copies, waits for them, and re-layouts  60 us
    dot_general x4, matrix products, lag_window(): jnp.einsum('nt,nlt->nl', left_rows, windows, preferred_element_type=jnp.f...  47.4 us
  transfers between devices with their start and end apart: 4, of which 4 were waited for; matrix products, arithmetic and copies ran while one was open for 0% of the time, Pallas kernels for 0%

commit v1 on v0

--- a/solution.py
+++ b/solution.py
@@ -86,7 +86,9 @@
     centred, padded = shard_prelude(
         spike_sample, spike_unit, spike_amp, group_index, shard_index, shard_count
     )
-    summed = lax.psum(pair_terms(centred, padded, first_units, second_units), "tm")
+    summed = jnp.sum(
+        lax.all_gather(pair_terms(centred, padded, first_units, second_units), "tm"), axis=0
+    )
     return lax.dynamic_slice_in_dim(summed, shard_index * per_shard, per_shard, 1)
 
 

time: 397 us -> 373 us (0.940)
  the two profiles are of different devices: /device:TPU:8 before, /device:TPU:1 now
where the time goes in v1:
time: 373 us; the launch traced here: 372 us
  waiting for transfers between devices  136 us (36%)
  local copies, waits for them, and re-layouts  71.6 us (19%)
  blocking collectives  67.5 us (18%)
  matrix products  49.1 us (13%)
  starting transfers between devices  19.4 us (5%)
  between operations  13.5 us (4%)
  other arithmetic  11.5 us (3%)
    all_gather x1, waiting for transfers between devices, local(): lax.all_gather(pair_terms(centred, padded, first_units, second_units), 'tm')  130 us
    psum x1, blocking collectives, shard_prelude(): totals = lax.psum(jnp.sum(trains, axis=1), 'tm')  67.5 us
    while x408, local copies, waits for them, and re-layouts  60 us
    dot_general x4, matrix products, lag_window(): jnp.einsum('nt,nlt->nl', left_rows, windows, preferred_element_type=jnp.f...  47.4 us
    ppermute x1, starting transfers between devices, passed_along(): return lax.ppermute(array, axis, pairs)  16.8 us
  transfers between devices with their start and end apart: 4, of which 3 were waited for; matrix products, arithmetic and copies ran while one was open for 0% of the time, Pallas kernels for 0%

profile of v1, /device:TPU:1, one launch (start us, length us, event | category | flops | bytes accessed | tf_op | source)
XLA Modules:
  0.0 372.4 jit_solution(17425031360348410562)
XLA Ops:
  6.5 0.8 broadcast_divide_fusion
  7.3 0.8 and_reduce_fusion
  8.1 0.7 broadcast_subtract_fusion
  8.9 0.8 reduce.3
  9.7 1.7 fusion.13
  11.3 67.5 %psum.7 = f32[384]{0:T(512)S(1)} all-reduce(f32[384]{0:T(512)S(1)} %get-tuple-element.60), channel_id=1, replica_groups=mesh['chan'=16,'tm'=32] {'tm'}, use_global_device_ids=true, to_apply=%region_1.2 | all-reduce | flops 384 | bytes 3072 | tf_op jit(solution)/shard_map/psum | solution.py:70
  78.8 0.1 subtract_convert_fusion
  79.0 16.8 %collective-permute-start = (bf16[64,256]{1,0:T(8,128)(2,1)S(1)}, bf16[64,256]{1,0:T(8,128)(2,1)S(1)}, u32[]{:S(2)}, u32[]{:S(2)}) collective-permute-start(bf16[64,256]{1,0:T(8,128)(2,1)S(1)} %slice.428), channel_id=1, source_target_pairs={{32,0},{64,32},{96,64},{128,96},{160,128},{192,160},{224,192},{256... | collective-permute-start | bytes 98312 | tf_op jit(solution)/shard_map/ppermute | solution.py:17
  95.7 2.8 collective-permute-done
  98.6 1.3 collective-permute-start.1
  99.9 1.3 collective-permute-start.2
  101.2 0.8 subtract_reduce_fusion
  102.1 3.5 collective-permute-done.2
  105.6 0.2 pad_maximum_fusion
  105.8 121.6 %while.10 = (s32[]{:T(128)}, f32[4,256,101]{2,1,0:T(8,128)S(1)}, s32[4,256]{1,0:T(4,128)S(1)}, bf16[384,256]{1,0:T(8,128)(2,1)S(1)}, s32[4,256]{1,0:T(4,128)S(1)}, /*index=5*/bf16[448,356]{1,0:T(8,128)(2,1)S(1)}, s32[]{:T(128)}) while((s32[]{:T(128)}, f32[4,256,101]{2,1,0:T(8,128)S(1)}, s32[4,256]{1,0:T(4,128)S(1)}, ...), condition=%wide.region_3.4_spmd, body=%wide.region_2.3_spmd.sunk | while | flops 13401602 | bytes 94439536 | solution.py:52
  106.0 1.2 gather_fusion
  107.2 0.1 broadcast_select_fusion.2
  108.0 0.1 constant_dynamic-update-slice_fusion.209
  108.1 0.1 constant_dynamic-update-slice_fusion.210
  108.2 0.1 constant_dynamic-update-slice_fusion.211
  108.3 0.1 constant_dynamic-update-slice_fusion.212
  108.4 0.1 constant_dynamic-update-slice_fusion.213
  108.5 0.1 constant_dynamic-update-slice_fusion.214
  108.7 0.1 constant_dynamic-update-slice_fusion.215
  108.8 0.1 constant_dynamic-update-slice_fusion.216
  108.9 0.1 constant_dynamic-update-slice_fusion.217
  118.5 4.7 %copy-done = bf16[256,101,256]{2,0,1:T(8,128)(2,1)} copy-done((bf16[256,101,256]{2,0,1:T(8,128)(2,1)}, bf16[256,101,256]{2,0,1:T(8,128)(2,1)S(1)}, u32[]{:S(2)}) %copy-start) | copy-done | bytes 13238296 | tf_op jit(solution)/shard_map/while
  123.2 1.1 gather_fusion.1
  124.5 11.8 %fusion.19 = f32[256,1,101]{2,1,0:T(1,128)S(1)} fusion(bf16[256,101,256]{2,0,1:T(8,128)(2,1)} %copy-done, bf16[256,256,1]{1,0,2:T(8,128)(2,1)S(1)} %select_bitcast_fusion.2), kind=kOutput, calls=%fused_computation.2.clone.1 | convolution fusion | flops 13238272 | bytes 13472768 | tf_op jit(solution)/shard_map/while/body/eval_jaxpr/nt,nlt->nl/dot_general | solution.py:40
  136.4 1.2 gather_fusion
  137.5 0.1 broadcast_select_fusion.2
  148.9 4.7 %copy-done = bf16[256,101,256]{2,0,1:T(8,128)(2,1)} copy-done((bf16[256,101,256]{2,0,1:T(8,128)(2,1)}, bf16[256,101,256]{2,0,1:T(8,128)(2,1)S(1)}, u32[]{:S(2)}) %copy-start) | copy-done | bytes 13238296 | tf_op jit(solution)/shard_map/while
  153.5 1.1 gather_fusion.1
  154.8 11.8 %fusion.19 = f32[256,1,101]{2,1,0:T(1,128)S(1)} fusion(bf16[256,101,256]{2,0,1:T(8,128)(2,1)} %copy-done, bf16[256,256,1]{1,0,2:T(8,128)(2,1)S(1)} %select_bitcast_fusion.2), kind=kOutput, calls=%fused_computation.2.clone.1 | convolution fusion | flops 13238272 | bytes 13472768 | tf_op jit(solution)/shard_map/while/body/eval_jaxpr/nt,nlt->nl/dot_general | solution.py:40
  166.7 1.2 gather_fusion
  167.9 0.1 broadcast_select_fusion.2
  179.2 4.7 %copy-done = bf16[256,101,256]{2,0,1:T(8,128)(2,1)} copy-done((bf16[256,101,256]{2,0,1:T(8,128)(2,1)}, bf16[256,101,256]{2,0,1:T(8,128)(2,1)S(1)}, u32[]{:S(2)}) %copy-start) | copy-done | bytes 13238296 | tf_op jit(solution)/shard_map/while
  183.9 1.1 gather_fusion.1
  185.2 11.8 %fusion.19 = f32[256,1,101]{2,1,0:T(1,128)S(1)} fusion(bf16[256,101,256]{2,0,1:T(8,128)(2,1)} %copy-done, bf16[256,256,1]{1,0,2:T(8,128)(2,1)S(1)} %select_bitcast_fusion.2), kind=kOutput, calls=%fused_computation.2.clone.1 | convolution fusion | flops 13238272 | bytes 13472768 | tf_op jit(solution)/shard_map/while/body/eval_jaxpr/nt,nlt->nl/dot_general | solution.py:40
  197.1 1.2 gather_fusion
  198.3 0.1 broadcast_select_fusion.2
  209.6 4.7 %copy-done = bf16[256,101,256]{2,0,1:T(8,128)(2,1)} copy-done((bf16[256,101,256]{2,0,1:T(8,128)(2,1)}, bf16[256,101,256]{2,0,1:T(8,128)(2,1)S(1)}, u32[]{:S(2)}) %copy-start) | copy-done | bytes 13238296 | tf_op jit(solution)/shard_map/while
  214.3 1.1 gather_fusion.1
  215.6 11.8 %fusion.19 = f32[256,1,101]{2,1,0:T(1,128)S(1)} fusion(bf16[256,101,256]{2,0,1:T(8,128)(2,1)} %copy-done, bf16[256,256,1]{1,0,2:T(8,128)(2,1)S(1)} %select_bitcast_fusion.2), kind=kOutput, calls=%fused_computation.2.clone.1 | convolution fusion | flops 13238272 | bytes 13472768 | tf_op jit(solution)/shard_map/while/body/eval_jaxpr/nt,nlt->nl/dot_general | solution.py:40
  227.4 1.0 copy.11
  228.4 130.1 %all-gather.4.cloned.1.call-done = f32[32,101,1024]{2,1,0:T(8,128)} async-done(((f32[1,101,1024]{2,1,0:T(8,128)}), f32[32,101,1024]{2,1,0:T(8,128)}) %all-gather.4.cloned.1.call-update) | async-done | bytes 13238288 | tf_op jit(solution)/shard_map/all_gather | solution.py:90
  358.6 6.2 %reduce_sum.19 = f32[101,1024]{1,0:T(8,128)S(1)} reduce(f32[32,101,1024]{2,1,0:T(8,128)} %all-gather.4.cloned.1.call-done, f32[]{:T(128)} %constant.63.clone.1), dimensions={0}, to_apply=%region_4.5 | reduce | flops 3206144 | bytes 13651972 | tf_op jit(solution)/shard_map/reduce_sum | solution.py:89
  364.9 0.7 copy.7
  (438 shorter events, 41.7 us)
Async XLA Ops:
  6.5 352.0 %all-gather.4.cloned.1.call-start = ((), (), s32[]{:S(2)}) async-start(), calls=%async_computation | async-start | bytes 14057472 | tf_op jit(solution)/shard_map/all_gather | solution.py:90
  79.0 19.5 %collective-permute-start = (bf16[64,256]{1,0:T(8,128)(2,1)S(1)}, bf16[64,256]{1,0:T(8,128)(2,1)S(1)}, u32[]{:S(2)}, u32[]{:S(2)}) collective-permute-start(bf16[64,256]{1,0:T(8,128)(2,1)S(1)} %slice.428), channel_id=1, source_target_pairs={{32,0},{64,32},{96,64},{128,96},{160,128},{192,160},{224,192},{256... | collective-permute-start | bytes 98312 | tf_op jit(solution)/shard_map/ppermute | solution.py:17
  98.6 3.4 collective-permute-start.1
  99.9 5.6 %collective-permute-start.2 = (bf16[448,50]{1,0:T(8,128)(2,1)S(1)}, bf16[448,50]{1,0:T(8,128)(2,1)S(1)}, u32[]{:S(2)}, u32[]{:S(2)}) collective-permute-start(bf16[448,50]{1,0:T(8,128)(2,1)S(1)} %get-tuple-element.59), channel_id=1, source_target_pairs={{1,0},{2,1},{3,2},{4,3},{5,4},{6,5},{7,6},{8,7},{9,8},{10,9},{11,1... | collective-permute-start | bytes 134408 | tf_op jit(solution)/shard_map/ppermute | solution.py:30
  118.5 4.7 %copy-start = (bf16[256,101,256]{2,0,1:T(8,128)(2,1)}, bf16[256,101,256]{2,0,1:T(8,128)(2,1)S(1)}, u32[]{:S(2)}) copy-start(bf16[256,101,256]{2,0,1:T(8,128)(2,1)S(1)} %constant_dynamic-update-slice_fusion.302) | copy-start | bytes 39714820 | tf_op jit(solution)/shard_map/while
  148.8 4.7 %copy-start = (bf16[256,101,256]{2,0,1:T(8,128)(2,1)}, bf16[256,101,256]{2,0,1:T(8,128)(2,1)S(1)}, u32[]{:S(2)}) copy-start(bf16[256,101,256]{2,0,1:T(8,128)(2,1)S(1)} %constant_dynamic-update-slice_fusion.302) | copy-start | bytes 39714820 | tf_op jit(solution)/shard_map/while
  179.2 4.7 %copy-start = (bf16[256,101,256]{2,0,1:T(8,128)(2,1)}, bf16[256,101,256]{2,0,1:T(8,128)(2,1)S(1)}, u32[]{:S(2)}) copy-start(bf16[256,101,256]{2,0,1:T(8,128)(2,1)S(1)} %constant_dynamic-update-slice_fusion.302) | copy-start | bytes 39714820 | tf_op jit(solution)/shard_map/while
  209.6 4.7 %copy-start = (bf16[256,101,256]{2,0,1:T(8,128)(2,1)}, bf16[256,101,256]{2,0,1:T(8,128)(2,1)S(1)}, u32[]{:S(2)}) copy-start(bf16[256,101,256]{2,0,1:T(8,128)(2,1)S(1)} %constant_dynamic-update-slice_fusion.302) | copy-start | bytes 39714820 | tf_op jit(solution)/shard_map/while
Sparse Core Ops, SparseCore 0:
  228.6 129.9 all-gather.3
